TPU v7x, 128 devices: a whole 4x4x4 slice. The times are simulated.
128 devices in a mesh: dp: 8 (over x, core), pair: 16 (over z, y).
Axes of the slice: x: 4, y: 4, z: 4, core: 2. Of those that a mesh axis runs over, the one named last changes fastest.
Arguments:
- anchor: bfloat16 [5, 4096, 1024], P(None, ('dp', 'pair')), may hold values from -20 to 20
- partner: bfloat16 [5, 4096, 1024], P(None, ('dp', 'pair')), may hold values from -12 to 12
- counts: int32 [5], replicated, may hold values from 512 to 4096, as said below
- pair_scale: float32 [5], replicated, may hold values from 2 to 8
Outputs:
- loss_value: float32 [], replicated
- grad_anchor: float32 [5, 4096, 1024], P(None, ('dp', 'pair'))
- grad_partner: float32 [5, 4096, 1024], P(None, ('dp', 'pair'))
Inputs may be any that keep to these rules, and one draw needn't show every extreme that they name: The valid samples of pair p are its rows 0 to counts[p] - 1; one pair has all 4096 rows valid.
All inputs are finite; a program needn't handle non-finite values.
Results may differ from a plain program's by a relative error of at most 0.0021.
Values may be sent and summed in bfloat16 or wider, within the bound.
No kernel may reach another device: no remote copies, remote signals or barrier semaphores. Data moves between devices by JAX's collectives and lax.ppermute only.
A program may use at most 128 MiB of HBM per device.

v0:
```python
import math
import jax
import jax.numpy as jnp
from jax import lax
from jax.sharding import PartitionSpec as P

NEG = -1e30


def merge_gathered(stats):
    highs = stats[:, 0]
    sums = stats[:, 1]
    highest = jnp.max(highs, axis=0)
    summed = jnp.sum(sums * jnp.exp(highs - highest[None]), axis=0)
    return (highest, summed)


def per_device(anchor, partner, counts, pair_scale):
    pair_count, shard_rows, model_width = anchor.shape
    score_scale = 4.0 / math.sqrt(model_width)
    dp_size = lax.axis_size("dp")
    pair_size = lax.axis_size("pair")
    dp_index = lax.axis_index("dp")
    pair_place = lax.axis_index("pair")
    own_first = (dp_index * pair_size + pair_place) * shard_rows
    row_set = lax.all_gather(anchor, "pair", axis=1, tiled=True)
    col_set = lax.all_gather(partner, "dp", axis=1, tiled=True)
    row_count = row_set.shape[1]
    offsets = jnp.arange(shard_rows, dtype=jnp.int32)
    row_global = dp_index * row_count + jnp.arange(row_count, dtype=jnp.int32)
    col_first = (jnp.arange(dp_size, dtype=jnp.int32) * pair_size + pair_place) * shard_rows
    col_global = (col_first[:, None] + offsets[None, :]).reshape(-1)
    row_valid = row_global[None, :] < counts[:, None]
    col_valid = col_global[None, :] < counts[:, None]
    inside = row_valid[:, :, None] & col_valid[:, None, :]
    scores = (
        jnp.einsum("prd,pcd->prc", row_set, col_set, preferred_element_type=jnp.float32)
        * score_scale
    )
    masked = jnp.where(inside, scores, NEG)
    row_high = jnp.max(masked, axis=2)
    row_sum = jnp.sum(jnp.where(inside, jnp.exp(masked - row_high[:, :, None]), 0.0), axis=2)
    col_high = jnp.max(masked, axis=1)
    col_sum = jnp.sum(jnp.where(inside, jnp.exp(masked - col_high[:, None, :]), 0.0), axis=1)
    row_stats = lax.all_gather(jnp.stack([row_high, row_sum]), "pair")
    col_stats = lax.all_gather(jnp.stack([col_high, col_sum]), "dp")
    row_high, row_sum = merge_gathered(row_stats)
    col_high, col_sum = merge_gathered(col_stats)
    row_lse = jnp.where(row_valid, row_high + jnp.log(jnp.where(row_valid, row_sum, 1.0)), 0.0)
    col_lse = jnp.where(col_valid, col_high + jnp.log(jnp.where(col_valid, col_sum, 1.0)), 0.0)
    own_valid = own_first + offsets[None, :] < counts[:, None]
    row_own = lax.dynamic_slice_in_dim(row_lse, pair_place * shard_rows, shard_rows, 1)
    col_own = lax.dynamic_slice_in_dim(col_lse, dp_index * shard_rows, shard_rows, 1)
    positive = (
        jnp.sum(anchor.astype(jnp.float32) * partner.astype(jnp.float32), axis=2) * score_scale
    )
    loss_terms = jnp.where(own_valid, row_own + col_own - 2.0 * positive, 0.0)
    totals = lax.psum(jnp.sum(loss_terms, axis=1), ("dp", "pair"))
    loss_value = jnp.sum(totals / (2.0 * counts.astype(jnp.float32))) / pair_count
    prob_row = jnp.where(inside, jnp.exp(scores - row_lse[:, :, None]), 0.0)
    prob_col = jnp.where(inside, jnp.exp(scores - col_lse[:, None, :]), 0.0)
    weights = (pair_scale[:, None, None] * 0.5 * (prob_row + prob_col)).astype(jnp.bfloat16)
    grad_rows = (
        jnp.einsum("prc,pcd->prd", weights, col_set, preferred_element_type=jnp.float32)
        * score_scale
    )
    grad_cols = (
        jnp.einsum("prc,prd->pcd", weights, row_set, preferred_element_type=jnp.float32)
        * score_scale
    )
    anchor_part = lax.psum_scatter(grad_rows, "pair", scatter_dimension=1, tiled=True)
    partner_part = lax.psum_scatter(grad_cols, "dp", scatter_dimension=1, tiled=True)
    own_term = (pair_scale * score_scale)[:, None, None]
    keep_rows = own_valid[:, :, None]
    anchor_out = jnp.where(keep_rows, anchor_part - own_term * partner.astype(jnp.float32), 0.0)
    partner_out = jnp.where(keep_rows, partner_part - own_term * anchor.astype(jnp.float32), 0.0)
    return (loss_value, anchor_out, partner_out)


def solution(mesh):
    in_specs = (P(None, ("dp", "pair"), None), P(None, ("dp", "pair"), None), P(), P())
    out_specs = (P(), P(None, ("dp", "pair"), None), P(None, ("dp", "pair"), None))
    return jax.shard_map(
        per_device, mesh=mesh, in_specs=in_specs, out_specs=out_specs, check_vma=False
    )
```

profile of v0, /device:TPU:1, one launch (start us, length us, event | category | flops | bytes accessed | tf_op | source)
XLA Modules:
  0.0 354.5 jit_solution(2730051306671288347)
XLA Ops:
  7.2 0.0 all-gather.7.cloned.1.call-start
  7.2 0.7 all-gather.7.cloned.1.call-update
  7.9 0.0 all-gather.5.cloned.1.call-start
  7.9 0.7 all-gather.5.cloned.1.call-update
  8.6 0.0 reduce-scatter.5.cloned.1.call-start
  8.7 0.1 iota_add_fusion
  8.8 0.1 add.96
  8.9 0.7 broadcast_multiply_fusion.2
  9.5 0.7 broadcast_compare_fusion.1
  10.3 0.7 broadcast_compare_fusion
  11.0 28.5 %all-gather.7.cloned.1.call-done = bf16[5,256,1024]{2,1,0:T(8,128)(2,1)} async-done(((bf16[5,32,1024]{2,1,0:T(8,128)(2,1)}), bf16[5,256,1024]{2,1,0:T(8,128)(2,1)}) %all-gather.7.cloned.1.call-update) | async-done | bytes 2621456 | tf_op jit(solution)/shard_map/all_gather | solution.py:27
  39.4 58.8 %all-gather.5.cloned.1.call-done = bf16[5,512,1024]{2,1,0:T(8,128)(2,1)} async-done(((bf16[5,32,1024]{2,1,0:T(8,128)(2,1)}), bf16[5,512,1024]{2,1,0:T(8,128)(2,1)}) %all-gather.5.cloned.1.call-update) | async-done | bytes 5242896 | tf_op jit(solution)/shard_map/all_gather | solution.py:26
  98.2 4.9 %fusion.6 = (f32[5,512]{1,0:T(8,128)S(1)}, f32[5,256]{1,0:T(8,128)S(1)}, f32[5,512,256]{2,1,0:T(8,128)S(1)}) fusion(pred[5,256]{1,0:T(8,128)(4,1)S(1)} %broadcast_compare_fusion.1, pred[5,512]{1,0:T(8,128)(4,1)S(1)} %broadcast_compare_fusion, bf16[5,512,1024]{2,1,0:T(8,128)(2,1)} %all-gather.5.cloned.1.call-done, ...), kind=kOutput, calls=%fused_computation.13 | convolution fusion | flops 1345450240 | bytes 10504960 | tf_op jit(solution)/shard_map/prd,pcd->prc/dot_general | solution.py:37
  103.2 0.0 copy-start.2
  103.2 2.0 fusion
  105.2 13.6 %all-gather.1 = f32[16,5,256]{2,1,0:T(8,128)S(1)} all-gather(f32[2,5,256]{2,1,0:T(8,128)S(1)} %pad_maximum_fusion.1), channel_id=3, replica_groups=mesh['dp'=8,'pair'=16] {'dp'}, dimensions={0}, use_global_device_ids=true | all-gather | bytes 92160 | tf_op jit(solution)/shard_map/all_gather | solution.py:46
  118.9 0.1 add_select_fusion.1
  119.0 18.7 %all-gather = f32[32,5,512]{2,1,0:T(8,128)S(1)} all-gather(f32[2,5,512]{2,1,0:T(8,128)S(1)} %pad_maximum_fusion), channel_id=2, replica_groups=mesh['dp'=8,'pair'=16] {'pair'}, dimensions={0}, use_global_device_ids=true | all-gather | bytes 348160 | tf_op jit(solution)/shard_map/all_gather | solution.py:45
  137.7 0.1 fusion.13
  137.8 0.1 add_select_fusion
  137.8 5.1 %broadcast_multiply_fusion.1 = f32[5,256,1024]{2,1,0:T(8,128)} fusion(bf16[5,512,1024]{2,1,0:T(8,128)(2,1)S(1)} %copy-done.3, f32[5,512,256]{2,1,0:T(8,128)S(1)} %get-tuple-element.12, f32[5,256]{1,0:T(8,128)S(1)} %add_select_fusion.1, f32[5,512]{1,0:T(8,128)S(1)} %add_select_fusion, f32[5]{0:T(128)S(1)} %get-tuple-element.11, ...), kind=kOutput, calls=%fused_computation.11 | convolution fusion | flops 1349386240 | bytes 13126420 | tf_op jit(solution)/shard_map/prc,prd->pcd/dot_general | solution.py:68
  142.9 0.0 reduce-scatter.5.cloned.1.call-update
  142.9 0.0 reduce-scatter.3.cloned.1.call-start
  143.0 7.6 %broadcast_multiply_fusion = f32[5,512,1024]{2,1,0:T(8,128)} fusion(bf16[5,256,1024]{2,1,0:T(8,128)(2,1)} %all-gather.7.cloned.1.call-done, f32[5,512,256]{2,1,0:T(8,128)S(1)} %get-tuple-element.12, f32[5,256]{1,0:T(8,128)S(1)} %add_select_fusion.1, f32[5,512]{1,0:T(8,128)S(1)} %add_select_fusion, f32[5]{0:T(128)S(1)} %get-tuple-element.11, ...), kind=kOutput, calls=%fused_computation.5 | convolution fusion | flops 1350696960 | bytes 15747860 | tf_op jit(solution)/shard_map/prc,pcd->prd/dot_general | solution.py:64
  150.6 0.0 reduce-scatter.3.cloned.1.call-update
  150.6 0.1 broadcast_compare_fusion.2
  150.7 32.2 %reduce-scatter.5.cloned.1.call-done = f32[5,32,1024]{2,1,0:T(8,128)} async-done(((f32[5,256,1024]{2,1,0:T(8,128)}), f32[5,32,1024]{2,1,0:T(8,128)}) %reduce-scatter.5.cloned.1.call-update) | async-done | bytes 655376 | tf_op jit(solution)/shard_map/reduce_scatter | solution.py:72
  182.9 94.8 %reduce-scatter.3.cloned.1.call-done = f32[5,32,1024]{2,1,0:T(8,128)} async-done(((f32[5,512,1024]{2,1,0:T(8,128)}), f32[5,32,1024]{2,1,0:T(8,128)}) %reduce-scatter.3.cloned.1.call-update) | async-done | bytes 655376 | tf_op jit(solution)/shard_map/reduce_scatter | solution.py:71
  277.7 2.7 fusion.8
  280.4 0.2 select_reduce_fusion
  280.6 65.0 %psum.7 = f32[5]{0:T(128)S(1)} all-reduce(f32[5]{0:T(128)S(1)} %select_reduce_fusion), channel_id=1, replica_groups=mesh['dp'=8,'pair'=16] {'dp','pair'}, use_global_device_ids=true, to_apply=%region_10.11 | all-reduce | flops 5 | bytes 40 | tf_op jit(solution)/shard_map/psum | solution.py:58
  345.6 0.6 fusion.18
  (15 shorter events, 0.1 us)
Async XLA Ops:
  7.2 32.3 %all-gather.7.cloned.1.call-start = ((), (), s32[]{:S(2)}) async-start(), calls=%async_computation.3 | async-start | bytes 2949120 | tf_op jit(solution)/shard_map/all_gather | solution.py:27
  7.9 90.3 %all-gather.5.cloned.1.call-start = ((), (), s32[]{:S(2)}) async-start(), calls=%async_computation.2 | async-start | bytes 5570560 | tf_op jit(solution)/shard_map/all_gather | solution.py:26
  8.6 174.2 %reduce-scatter.5.cloned.1.call-start = ((), (), s32[]{:S(2)}) async-start(), calls=%async_computation.5 | async-start | bytes 5898240 | tf_op jit(solution)/shard_map/reduce_scatter | solution.py:72
  98.2 39.6 %copy-start.3 = (bf16[5,512,1024]{2,1,0:T(8,128)(2,1)S(1)}, bf16[5,512,1024]{2,1,0:T(8,128)(2,1)}, u32[]{:S(2)}) copy-start(bf16[5,512,1024]{2,1,0:T(8,128)(2,1)} %all-gather.5.cloned.1.call-done) | copy-start | bytes 15728644
  103.2 15.7 %copy-start.2 = (s32[5]{0:T(128)S(1)}, s32[5]{0:T(128)}, u32[]{:S(2)}) copy-start(s32[5]{0:T(128)} %param.6) | copy-start | bytes 64
  142.9 134.8 %reduce-scatter.3.cloned.1.call-start = ((), (), s32[]{:S(2)}) async-start(), calls=%async_computation.4 | async-start | bytes 11141120 | tf_op jit(solution)/shard_map/reduce_scatter | solution.py:71
  150.5 127.1 %copy-start = (bf16[5,32,1024]{2,1,0:T(8,128)(2,1)S(1)}, bf16[5,32,1024]{2,1,0:T(8,128)(2,1)}, u32[]{:S(2)}) copy-start(bf16[5,32,1024]{2,1,0:T(8,128)(2,1)} %param.5) | copy-start | bytes 983044
  150.5 127.1 %copy-start.1 = (bf16[5,32,1024]{2,1,0:T(8,128)(2,1)S(1)}, bf16[5,32,1024]{2,1,0:T(8,128)(2,1)}, u32[]{:S(2)}) copy-start(bf16[5,32,1024]{2,1,0:T(8,128)(2,1)} %param.4) | copy-start | bytes 983044
Sparse Core Ops, SparseCore 0:
  9.7 29.7 all-gather.6
  41.6 56.6 all-gather.4
  143.0 39.7 reduce-scatter.4
  186.2 91.4 reduce-scatter.2
where the time goes:
time: 355 us
  waiting for transfers between devices  216 us (61%)
  blocking collectives  97.3 us (27%)
  matrix products  17.6 us (5%)
  between operations  15.6 us (4%)
  other arithmetic  8.11 us (2%)
    reduce_scatter x1, waiting for transfers between devices, per_device(): lax.psum_scatter(grad_rows, 'pair', scatter_dimension=1, tiled=True)  94.8 us
    psum x1, blocking collectives, per_device(): totals = lax.psum(jnp.sum(loss_terms, axis=1), ('dp', 'pair'))  65 us
    all_gather x1, waiting for transfers between devices, per_device(): row_set = lax.all_gather(anchor, 'pair', axis=1, tiled=True)  58.8 us
    reduce_scatter x1, waiting for transfers between devices, per_device(): lax.psum_scatter(grad_cols, 'dp', scatter_dimension=1, tiled=True)  32.2 us
    all_gather x1, waiting for transfers between devices, per_device(): col_set = lax.all_gather(partner, 'dp', axis=1, tiled=True)  28.5 us
    all_gather x1, blocking collectives, per_device(): row_stats = lax.all_gather(jnp.stack([row_high, row_sum]), 'pair')  18.7 us
    all_gather x1, blocking collectives, per_device(): col_stats = lax.all_gather(jnp.stack([col_high, col_sum]), 'dp')  13.6 us
    dot_general x1, matrix products, per_device(): jnp.einsum('prc,pcd->prd', weights, col_set, preferred_element_type=jnp.f...  7.57 us
  transfers between devices with their start and end apart: 4, of which 4 were waited for; matrix products, arithmetic and copies ran while one was open for 3% of the time, Pallas kernels for 0%

commit v1 on v0

--- a/solution.py
+++ b/solution.py
@@ -5,6 +5,11 @@
 from jax.sharding import PartitionSpec as P
 
 NEG = -1e30
+
+
+def by_each_axis(x, axis_one, axis_two):
+    partial = lax.psum(x, axis_one)
+    return lax.psum(partial, axis_two)
 
 
 def merge_gathered(stats):
@@ -55,7 +60,7 @@
         jnp.sum(anchor.astype(jnp.float32) * partner.astype(jnp.float32), axis=2) * score_scale
     )
     loss_terms = jnp.where(own_valid, row_own + col_own - 2.0 * positive, 0.0)
-    totals = lax.psum(jnp.sum(loss_terms, axis=1), ("dp", "pair"))
+    totals = by_each_axis(jnp.sum(loss_terms, axis=1), "pair", "dp")
     loss_value = jnp.sum(totals / (2.0 * counts.astype(jnp.float32))) / pair_count
     prob_row = jnp.where(inside, jnp.exp(scores - row_lse[:, :, None]), 0.0)
     prob_col = jnp.where(inside, jnp.exp(scores - col_lse[:, None, :]), 0.0)

time: 355 us -> 341 us (0.961)
  blocking collectives: 97.3 us -> 83.5 us
    psum x1 -> x2, blocking collectives: 65 us -> 51.3 us  [the longest x1 30.9 us: by_each_axis(): partial = lax.psum(x, axis_one)]
where the time goes in v1:
time: 341 us
  waiting for transfers between devices  216 us (63%)
  blocking collectives  83.5 us (24%)
  matrix products  17.6 us (5%)
  between operations  15.6 us (5%)
  other arithmetic  8.11 us (2%)
    reduce_scatter x1, waiting for transfers between devices, per_device(): lax.psum_scatter(grad_rows, 'pair', scatter_dimension=1, tiled=True)  94.8 us
    all_gather x1, waiting for transfers between devices, per_device(): row_set = lax.all_gather(anchor, 'pair', axis=1, tiled=True)  58.8 us
    reduce_scatter x1, waiting for transfers between devices, per_device(): lax.psum_scatter(grad_cols, 'dp', scatter_dimension=1, tiled=True)  32.2 us
    psum x1, blocking collectives, by_each_axis(): partial = lax.psum(x, axis_one)  30.9 us
    all_gather x1, waiting for transfers between devices, per_device(): col_set = lax.all_gather(partner, 'dp', axis=1, tiled=True)  28.5 us
    psum x1, blocking collectives, by_each_axis(): return lax.psum(partial, axis_two)  20.4 us
    all_gather x1, blocking collectives, per_device(): row_stats = lax.all_gather(jnp.stack([row_high, row_sum]), 'pair')  18.7 us
    all_gather x1, blocking collectives, per_device(): col_stats = lax.all_gather(jnp.stack([col_high, col_sum]), 'dp')  13.6 us
  transfers between devices with their start and end apart: 4, of which 4 were waited for; matrix products, arithmetic and copies ran while one was open for 3% of the time, Pallas kernels for 0%

profile of v1, /device:TPU:1, one launch (start us, length us, event | category | flops | bytes accessed | tf_op | source)
XLA Modules:
  0.0 340.8 jit_solution(11090121848938104500)
XLA Ops:
  7.2 0.0 all-gather.7.cloned.1.call-start
  7.2 0.7 all-gather.7.cloned.1.call-update
  7.9 0.0 all-gather.5.cloned.1.call-start
  7.9 0.7 all-gather.5.cloned.1.call-update
  8.6 0.0 reduce-scatter.5.cloned.1.call-start
  8.7 0.1 iota_add_fusion
  8.8 0.1 add.98
  8.9 0.7 broadcast_multiply_fusion.2
  9.5 0.7 broadcast_compare_fusion.1
  10.3 0.7 broadcast_compare_fusion
  11.0 28.5 %all-gather.7.cloned.1.call-done = bf16[5,256,1024]{2,1,0:T(8,128)(2,1)} async-done(((bf16[5,32,1024]{2,1,0:T(8,128)(2,1)}), bf16[5,256,1024]{2,1,0:T(8,128)(2,1)}) %all-gather.7.cloned.1.call-update) | async-done | bytes 2621456 | tf_op jit(solution)/shard_map/all_gather | solution.py:32
  39.4 58.8 %all-gather.5.cloned.1.call-done = bf16[5,512,1024]{2,1,0:T(8,128)(2,1)} async-done(((bf16[5,32,1024]{2,1,0:T(8,128)(2,1)}), bf16[5,512,1024]{2,1,0:T(8,128)(2,1)}) %all-gather.5.cloned.1.call-update) | async-done | bytes 5242896 | tf_op jit(solution)/shard_map/all_gather | solution.py:31
  98.2 4.9 %fusion.6 = (f32[5,512]{1,0:T(8,128)S(1)}, f32[5,256]{1,0:T(8,128)S(1)}, f32[5,512,256]{2,1,0:T(8,128)S(1)}) fusion(pred[5,256]{1,0:T(8,128)(4,1)S(1)} %broadcast_compare_fusion.1, pred[5,512]{1,0:T(8,128)(4,1)S(1)} %broadcast_compare_fusion, bf16[5,512,1024]{2,1,0:T(8,128)(2,1)} %all-gather.5.cloned.1.call-done, ...), kind=kOutput, calls=%fused_computation.13 | convolution fusion | flops 1345450240 | bytes 10504960 | tf_op jit(solution)/shard_map/prd,pcd->prc/dot_general | solution.py:42
  103.2 2.0 fusion
  105.2 13.6 %all-gather.1 = f32[16,5,256]{2,1,0:T(8,128)S(1)} all-gather(f32[2,5,256]{2,1,0:T(8,128)S(1)} %pad_maximum_fusion.1), channel_id=3, replica_groups=mesh['dp'=8,'pair'=16] {'dp'}, dimensions={0}, use_global_device_ids=true | all-gather | bytes 92160 | tf_op jit(solution)/shard_map/all_gather | solution.py:51
  118.9 0.1 add_select_fusion.1
  119.0 18.7 %all-gather = f32[32,5,512]{2,1,0:T(8,128)S(1)} all-gather(f32[2,5,512]{2,1,0:T(8,128)S(1)} %pad_maximum_fusion), channel_id=2, replica_groups=mesh['dp'=8,'pair'=16] {'pair'}, dimensions={0}, use_global_device_ids=true | all-gather | bytes 348160 | tf_op jit(solution)/shard_map/all_gather | solution.py:50
  137.7 0.1 fusion.13
  137.8 0.1 add_select_fusion
  137.8 5.1 %broadcast_multiply_fusion.1 = f32[5,256,1024]{2,1,0:T(8,128)} fusion(bf16[5,512,1024]{2,1,0:T(8,128)(2,1)S(1)} %copy-done.3, f32[5,512,256]{2,1,0:T(8,128)S(1)} %get-tuple-element.12, f32[5,256]{1,0:T(8,128)S(1)} %add_select_fusion.1, f32[5,512]{1,0:T(8,128)S(1)} %add_select_fusion, f32[5]{0:T(128)S(1)} %get-tuple-element.11, ...), kind=kOutput, calls=%fused_computation.11 | convolution fusion | flops 1349386240 | bytes 13126420 | tf_op jit(solution)/shard_map/prc,prd->pcd/dot_general | solution.py:73
  142.9 0.0 reduce-scatter.5.cloned.1.call-update
  142.9 0.0 reduce-scatter.3.cloned.1.call-start
  143.0 7.6 %broadcast_multiply_fusion = f32[5,512,1024]{2,1,0:T(8,128)} fusion(bf16[5,256,1024]{2,1,0:T(8,128)(2,1)} %all-gather.7.cloned.1.call-done, f32[5,512,256]{2,1,0:T(8,128)S(1)} %get-tuple-element.12, f32[5,256]{1,0:T(8,128)S(1)} %add_select_fusion.1, f32[5,512]{1,0:T(8,128)S(1)} %add_select_fusion, f32[5]{0:T(128)S(1)} %get-tuple-element.11, ...), kind=kOutput, calls=%fused_computation.5 | convolution fusion | flops 1350696960 | bytes 15747860 | tf_op jit(solution)/shard_map/prc,pcd->prd/dot_general | solution.py:69
  150.6 0.0 reduce-scatter.3.cloned.1.call-update
  150.6 0.1 broadcast_compare_fusion.2
  150.7 32.2 %reduce-scatter.5.cloned.1.call-done = f32[5,32,1024]{2,1,0:T(8,128)} async-done(((f32[5,256,1024]{2,1,0:T(8,128)}), f32[5,32,1024]{2,1,0:T(8,128)}) %reduce-scatter.5.cloned.1.call-update) | async-done | bytes 655376 | tf_op jit(solution)/shard_map/reduce_scatter | solution.py:77
  182.9 94.8 %reduce-scatter.3.cloned.1.call-done = f32[5,32,1024]{2,1,0:T(8,128)} async-done(((f32[5,512,1024]{2,1,0:T(8,128)}), f32[5,32,1024]{2,1,0:T(8,128)}) %reduce-scatter.3.cloned.1.call-update) | async-done | bytes 655376 | tf_op jit(solution)/shard_map/reduce_scatter | solution.py:76
  277.7 2.7 fusion.8
  280.4 0.2 select_reduce_fusion
  280.6 30.9 %psum.14 = f32[5]{0:T(128)S(1)} all-reduce(f32[5]{0:T(128)S(1)} %select_reduce_fusion), channel_id=1, replica_groups=mesh['dp'=8,'pair'=16] {'pair'}, use_global_device_ids=true, to_apply=%region_10.11 | all-reduce | flops 5 | bytes 40 | tf_op jit(solution)/shard_map/psum | solution.py:11
  311.5 20.4 %psum.15 = f32[5]{0:T(128)S(1)} all-reduce(f32[5]{0:T(128)S(1)} %psum.14), channel_id=1, replica_groups=mesh['dp'=8,'pair'=16] {'dp'}, use_global_device_ids=true, to_apply=%region_11.12 | all-reduce | flops 5 | bytes 40 | tf_op jit(solution)/shard_map/psum | solution.py:12
  331.9 0.6 fusion.18
  (16 shorter events, 0.1 us)
Async XLA Ops:
  7.2 32.3 %all-gather.7.cloned.1.call-start = ((), (), s32[]{:S(2)}) async-start(), calls=%async_computation.3 | async-start | bytes 2949120 | tf_op jit(solution)/shard_map/all_gather | solution.py:32
  7.9 90.3 %all-gather.5.cloned.1.call-start = ((), (), s32[]{:S(2)}) async-start(), calls=%async_computation.2 | async-start | bytes 5570560 | tf_op jit(solution)/shard_map/all_gather | solution.py:31
  8.6 174.2 %reduce-scatter.5.cloned.1.call-start = ((), (), s32[]{:S(2)}) async-start(), calls=%async_computation.5 | async-start | bytes 5898240 | tf_op jit(solution)/shard_map/reduce_scatter | solution.py:77
  98.2 39.6 %copy-start.3 = (bf16[5,512,1024]{2,1,0:T(8,128)(2,1)S(1)}, bf16[5,512,1024]{2,1,0:T(8,128)(2,1)}, u32[]{:S(2)}) copy-start(bf16[5,512,1024]{2,1,0:T(8,128)(2,1)} %all-gather.5.cloned.1.call-done) | copy-start | bytes 15728644
  103.2 15.7 %copy-start.2 = (s32[5]{0:T(128)S(1)}, s32[5]{0:T(128)}, u32[]{:S(2)}) copy-start(s32[5]{0:T(128)} %param.6) | copy-start | bytes 64
  142.9 134.8 %reduce-scatter.3.cloned.1.call-start = ((), (), s32[]{:S(2)}) async-start(), calls=%async_computation.4 | async-start | bytes 11141120 | tf_op jit(solution)/shard_map/reduce_scatter | solution.py:76
  150.5 127.1 %copy-start = (bf16[5,32,1024]{2,1,0:T(8,128)(2,1)S(1)}, bf16[5,32,1024]{2,1,0:T(8,128)(2,1)}, u32[]{:S(2)}) copy-start(bf16[5,32,1024]{2,1,0:T(8,128)(2,1)} %param.5) | copy-start | bytes 983044
  150.5 127.1 %copy-start.1 = (bf16[5,32,1024]{2,1,0:T(8,128)(2,1)S(1)}, bf16[5,32,1024]{2,1,0:T(8,128)(2,1)}, u32[]{:S(2)}) copy-start(bf16[5,32,1024]{2,1,0:T(8,128)(2,1)} %param.4) | copy-start | bytes 983044
Sparse Core Ops, SparseCore 0:
  9.7 29.7 all-gather.6
  41.6 56.6 all-gather.4
  143.0 39.7 reduce-scatter.4
  186.2 91.4 reduce-scatter.2
